TPU v7x, 32 devices: a whole 2x2x4 slice. The times are simulated.
32 devices in a mesh: groups: 2 (over x), seq: 8 (over z, y), rep: 2 (over core).
Axes of the slice: x: 2, y: 2, z: 4, core: 2. Of those that a mesh axis runs over, the one named last changes fastest.
Arguments:
- inputs: bfloat16 [4, 4096, 1536], P(('groups', 'rep'), 'seq'), parts along dimension 0, may hold values from -6 to 6
- lengths: int32 [4], P(('groups', 'rep')), parts along dimension 0, may hold values from 2049 to 4096, as said below
- conv_weight: bfloat16 [3, 48, 1536], replicated, may hold values from -0.5 to 0.5
- point_weight: bfloat16 [1536, 1536], replicated, may hold values from -0.15625 to 0.15625
- cotangent: bfloat16 [4, 4096, 1536], P(('groups', 'rep'), 'seq'), parts along dimension 0, may hold values from -6 to 6
Outputs:
- output: bfloat16 [4, 4096, 1536], P(('groups', 'rep'), 'seq'), parts along dimension 0
- grad_inputs: bfloat16 [4, 4096, 1536], P(('groups', 'rep'), 'seq'), parts along dimension 0
- grad_point: float32 [3072, 1536], P(('groups', 'seq', 'rep')), parts along dimension 0
- grad_conv: float32 [6, 48, 1536], P('groups'), parts along dimension 0
There are 2 independent parts, one for each index of `groups`. A program takes and returns all parts, laid end to end along the dimension named above; an argument that names none is the same for every part. Nothing has to cross between parts.
Inputs may be any that keep to these rules, and one draw needn't show every extreme that they name: `lengths`: one sample in each draw has all 4096 bins valid.
All inputs are finite; a program needn't handle non-finite values.
Results may differ from a plain program's by a relative error of at most 0.0031.
Values may be sent and summed in bfloat16 or wider, within the bound.
No kernel may reach another device: no remote copies, remote signals or barrier semaphores. Data moves between devices by JAX's collectives and lax.ppermute only.
A program may use at most 128 MiB of HBM per device.

v0:
```python
import math
import jax
import jax.numpy as jnp
from jax import lax
from jax.sharding import PartitionSpec as P

GROUP_CHANNELS = 48
DILATION_STEP = 64


def with_halo(cells, sides, width):
    for axis, dim in sides:
        count = lax.axis_size(axis)
        ends = count - 1
        head = lax.slice_in_dim(cells, 0, width, axis=dim)
        tail = lax.slice_in_dim(cells, cells.shape[dim] - width, cells.shape[dim], axis=dim)
        cells = jnp.concatenate(
            [
                lax.ppermute(tail, axis, [(i, (i + 1) % count) for i in range(ends)]),
                cells,
                lax.ppermute(head, axis, [((i + 1) % count, i) for i in range(ends)]),
            ],
            axis=dim,
        )
    return cells


def gelu_pair(pre):
    cdf = 0.5 * (1.0 + jax.scipy.special.erf(pre * 0.7071067811865476))
    dens = jnp.exp(-0.5 * pre * pre) * 0.3989422804014327
    return (pre * cdf, cdf + pre * dens)


def conv_taps(padded_input, weight, sequence_length):
    group_count = weight.shape[2] // GROUP_CHANNELS
    total = jnp.zeros(
        (padded_input.shape[0], sequence_length, group_count, GROUP_CHANNELS), jnp.float32
    )
    for kernel_offset in range(3):
        segment_window = padded_input[
            :, kernel_offset * DILATION_STEP : kernel_offset * DILATION_STEP + sequence_length
        ].reshape(padded_input.shape[0], sequence_length, group_count, GROUP_CHANNELS)
        wk = weight[kernel_offset].reshape(GROUP_CHANNELS, group_count, GROUP_CHANNELS)
        total = total + jnp.einsum(
            "slgi,igj->slgj", segment_window, wk, preferred_element_type=jnp.float32
        )
    return total.reshape(padded_input.shape[0], sequence_length, group_count * GROUP_CHANNELS)


def transpose_taps(padded_input, weight, sequence_length):
    group_count = weight.shape[2] // GROUP_CHANNELS
    total = jnp.zeros(
        (padded_input.shape[0], sequence_length, group_count, GROUP_CHANNELS), jnp.float32
    )
    for kernel_offset in range(3):
        segment_window = padded_input[
            :,
            (2 - kernel_offset) * DILATION_STEP : (2 - kernel_offset) * DILATION_STEP
            + sequence_length,
        ].reshape(padded_input.shape[0], sequence_length, group_count, GROUP_CHANNELS)
        wk = weight[kernel_offset].reshape(GROUP_CHANNELS, group_count, GROUP_CHANNELS)
        total = total + jnp.einsum(
            "slgj,igj->slgi", segment_window, wk, preferred_element_type=jnp.float32
        )
    return total.reshape(padded_input.shape[0], sequence_length, group_count * GROUP_CHANNELS)


def weight_taps(input_padded, output_gradient, sequence_length):
    group_count = output_gradient.shape[2] // GROUP_CHANNELS
    grouped = output_gradient.reshape(
        output_gradient.shape[0], sequence_length, group_count, GROUP_CHANNELS
    )
    taps = []
    for kernel_offset in range(3):
        segment_window = input_padded[
            :, kernel_offset * DILATION_STEP : kernel_offset * DILATION_STEP + sequence_length
        ].reshape(output_gradient.shape[0], sequence_length, group_count, GROUP_CHANNELS)
        taps.append(
            jnp.einsum(
                "slgi,slgj->igj", segment_window, grouped, preferred_element_type=jnp.float32
            ).reshape(GROUP_CHANNELS, group_count * GROUP_CHANNELS)
        )
    return jnp.stack(taps)


def on_device(inputs, lengths, conv_weight, point_weight, cotangent):
    local_bins = inputs.shape[1]
    chans = inputs.shape[2]
    seq_count = lax.axis_size("seq")
    rep_count = lax.axis_size("rep")
    seq_index = lax.axis_index("seq")
    positions = seq_index * local_bins + jnp.arange(local_bins, dtype=jnp.int32)
    mask = (positions[None, :] < lengths[:, None]).astype(jnp.float32)
    mask3 = mask[:, :, None]
    masked_input = (inputs.astype(jnp.float32) * mask3).astype(jnp.bfloat16)
    scale = 1.0 / math.sqrt(rep_count * seq_count * local_bins)
    padded_input = with_halo(masked_input, (("seq", 1),), DILATION_STEP)
    pre = conv_taps(padded_input, conv_weight, local_bins)
    act_val, slope = gelu_pair(pre)
    act = (act_val * mask3).astype(jnp.bfloat16)
    act_rows = act.reshape(local_bins, chans)
    cot_rows = cotangent.reshape(local_bins, chans)
    proj = jnp.dot(act_rows, point_weight, preferred_element_type=jnp.float32).reshape(inputs.shape)
    output = (inputs.astype(jnp.float32) + proj).astype(jnp.bfloat16)
    back = lax.dot_general(
        cot_rows, point_weight, (((1,), (1,)), ((), ())), preferred_element_type=jnp.float32
    )
    preactivation_gradient = (back.reshape(inputs.shape) * slope * mask3).astype(jnp.bfloat16)
    padded_gradient = with_halo(preactivation_gradient, (("seq", 1),), DILATION_STEP)
    spread = transpose_taps(padded_gradient, conv_weight, local_bins)
    conv_local = weight_taps(padded_input, preactivation_gradient, local_bins)
    grad_conv = lax.psum(conv_local, ("seq", "rep")) * scale
    grad_inputs = (cotangent.astype(jnp.float32) + mask3 * spread).astype(jnp.bfloat16)
    grad_point = lax.psum_scatter(
        lax.dot_general(
            act_rows, cot_rows, (((0,), (0,)), ((), ())), preferred_element_type=jnp.float32
        ),
        ("seq", "rep"),
        scatter_dimension=0,
        tiled=True,
    )
    grad_point = grad_point * scale
    return (output, grad_inputs, grad_point, grad_conv)


def solution(mesh):
    return jax.shard_map(
        on_device,
        mesh=mesh,
        in_specs=(
            P(("groups", "rep"), "seq", None),
            P(("groups", "rep")),
            P(),
            P(),
            P(("groups", "rep"), "seq", None),
        ),
        out_specs=(
            P(("groups", "rep"), "seq", None),
            P(("groups", "rep"), "seq", None),
            P(("groups", "seq", "rep"), None),
            P("groups", None, None),
        ),
        check_vma=False,
    )
```

profile of v0, /device:TPU:0, one launch (start us, length us, event | category | flops | bytes accessed | tf_op | source)
XLA Modules:
  0.0 282.3 jit_solution(17731582967760469702)
XLA Ops:
  11.7 6.2 %collective-permute-start = (bf16[1,64,1536]{2,1,0:T(8,128)(2,1)}, bf16[1,64,1536]{2,1,0:T(8,128)(2,1)}, u32[]{:S(2)}, u32[]{:S(2)}) collective-permute-start(bf16[1,64,1536]{2,1,0:T(8,128)(2,1)} %get-tuple-element.11), channel_id=1, source_target_pairs={{0,2},{2,4},{4,6},{6,8},{8,10},{10,12},{12,14},{1,3},{3,5},{5,7},{... | collective-permute-start | bytes 589832 | tf_op jit(solution)/shard_map/ppermute | solution.py:19
  21.5 1.8 copy.35
  25.2 3.2 %fusion.29 = f32[32,512,48]{1,2,0:T(8,128)} fusion(bf16[48,32,48]{0,2,1:T(8,128)(2,1)} %bitcast.90, bf16[512,32,48]{0,2,1:T(8,128)(2,1)S(1)} %bitcast.73), kind=kOutput, calls=%fused_computation.48 | convolution fusion | flops 75497472 | bytes 4866048 | tf_op jit(solution)/shard_map/slgi,igj->slgj/dot_general | solution.py:44
  28.4 2.9 %pad_maximum_fusion.2 = (bf16[1,512,1536]{2,1,0:T(8,128)(2,1)}, bf16[1,512,1536]{2,1,0:T(8,128)(2,1)}) fusion(bf16[1,64,1536]{2,1,0:T(8,128)(2,1)} %collective-permute-done.1, bf16[1,512,1536]{2,1,0:T(8,128)(2,1)S(1)} %fusion.1, bf16[1,64,1536]{2,1,0:T(8,128)(2,1)} %collective-permute-done), kind=kLoop, calls=%fused_computation.21 | loop fusion | flops 6291456 | bytes 5111808 | tf_op jit(solution)/shard_map/concatenate | solution.py:17
  31.3 2.6 copy.38
  35.7 2.0 fusion.28
  38.7 2.2 add_add_fusion.1
  40.9 3.7 %copy.41 = f32[512,1536]{1,0:T(8,128)} copy(f32[512,1536]{0,1:T(8,128)} %bitcast.79) | data formatting | bytes 6291456 | tf_op jit(solution)/shard_map/reshape | solution.py:47
  44.6 7.0 %fusion.7 = bf16[512,1536]{1,0:T(8,128)(2,1)} fusion(f32[512,1536]{1,0:T(8,128)} %copy.41, bf16[1536,1536]{1,0:T(8,128)(2,1)} %param.8, bf16[1,512,1536]{2,1,0:T(8,128)(2,1)S(1)} %copy-done.10, f32[512]{0:T(512)S(1)} %fusion.16), kind=kOutput, calls=%fused_computation.18 | convolution fusion | flops 2424569856 | bytes 11012096 | tf_op jit(solution)/shard_map/dot_general | solution.py:105
  53.3 3.0 %fusion.27 = f32[32,48,48]{2,1,0:T(8,128)} fusion(bf16[512,32,48]{0,2,1:T(8,128)(2,1)S(1)} %bitcast.69, bf16[512,32,48]{0,2,1:T(8,128)(2,1)} %bitcast.77), kind=kOutput, calls=%fused_computation.46 | convolution fusion | flops 75497472 | bytes 3440640 | tf_op jit(solution)/shard_map/slgi,slgj->igj/dot_general | solution.py:79
  59.1 2.1 copy.52
  62.4 2.0 pad_maximum_fusion.4
  64.5 8.6 %fusion.8 = f32[1536,1536]{1,0:T(8,128)} fusion(bf16[1,512,1536]{2,1,0:T(8,128)(2,1)} %param.9, f32[1,512,1,1,1,1,1536]{1,6,5,4,3,2,0:T(8,128)} %bitcast.80, f32[512]{0:T(512)S(1)} %fusion.16), kind=kOutput, calls=%fused_computation.23 | convolution fusion | flops 2420637696 | bytes 14157824 | tf_op jit(solution)/shard_map/dot_general | solution.py:115
  74.6 4.2 %collective-permute-start.3 = (bf16[1,64,1536]{2,1,0:T(8,128)(2,1)S(1)}, bf16[1,64,1536]{2,1,0:T(8,128)(2,1)S(1)}, u32[]{:S(2)}, u32[]{:S(2)}) collective-permute-start(bf16[1,64,1536]{2,1,0:T(8,128)(2,1)S(1)} %get-tuple-element.6), channel_id=1, source_target_pairs={{0,2},{2,4},{4,6},{6,8},{8,10},{10,12},{12,14},{1,3},{3,5},{5,7},{... | collective-permute-start | bytes 589832 | tf_op jit(solution)/shard_map/ppermute | solution.py:19
  80.4 7.6 %fusion.2 = bf16[1,512,1536]{2,1,0:T(8,128)(2,1)} fusion(bf16[1,512,1536]{2,1,0:T(8,128)(2,1)} %param.5, bf16[1536,1536]{1,0:T(8,128)(2,1)} %param.8, f32[512,1536]{1,0:T(8,128)} %copy.41, f32[512]{0:T(512)S(1)} %fusion.16), kind=kOutput, calls=%fused_computation.7 | convolution fusion | flops 2422996992 | bytes 11012096 | tf_op jit(solution)/shard_map/dot_general | solution.py:103
  88.0 2.3 fusion.24
  91.7 2.6 copy.49
  97.5 2.3 add_add_fusion
  99.8 2.4 copy.51
  102.1 3.0 %add_convert_fusion = bf16[1,512,1536]{2,1,0:T(8,128)(2,1)} fusion(f32[1,512,1536]{2,1,0:T(8,128)S(1)} %copy.51, bf16[1,512,1536]{2,1,0:T(8,128)(2,1)} %param.9, f32[512]{0:T(512)S(1)} %fusion.16), kind=kLoop, calls=%fused_computation.13 | loop fusion | flops 3145728 | bytes 6293504 | tf_op jit(solution)/shard_map/convert_element_type | solution.py:113
  105.1 53.9 %all-reduce.2.cloned.1.call-done = f32[3,48,1536]{2,1,0:T(8,128)} async-done(((f32[3,48,1536]{2,1,0:T(8,128)}), f32[3,48,1536]{2,1,0:T(8,128)}) %all-reduce.2.cloned.1.call-update) | async-done | bytes 884752 | tf_op jit(solution)/shard_map/psum | solution.py:112
  159.1 2.2 broadcast_multiply_fusion
  161.2 112.3 %reduce-scatter.2.cloned.1.call-done = f32[96,1536]{1,0:T(8,128)} async-done(((f32[1536,1536]{1,0:T(8,128)}), f32[96,1536]{1,0:T(8,128)}) %reduce-scatter.2.cloned.1.call-update) | async-done | bytes 589840 | tf_op jit(solution)/shard_map/reduce_scatter | solution.py:114
  273.5 1.9 broadcast_multiply_fusion.1
  (49 shorter events, 25.5 us)
Async XLA Ops:
  7.2 151.9 %all-reduce.2.cloned.1.call-start = ((), (), s32[]{:S(2)}) async-start(), calls=%async_computation.2 | async-start | bytes 1769472 | tf_op jit(solution)/shard_map/psum | solution.py:112
  10.4 18.0 %collective-permute-start.1 = (bf16[1,64,1536]{2,1,0:T(8,128)(2,1)}, bf16[1,64,1536]{2,1,0:T(8,128)(2,1)}, u32[]{:S(2)}, u32[]{:S(2)}) collective-permute-start(bf16[1,64,1536]{2,1,0:T(8,128)(2,1)} %get-tuple-element.10), channel_id=1, source_target_pairs={{2,0},{4,2},{6,4},{8,6},{10,8},{12,10},{14,12},{3,1},{5,3},{7,5},{... | collective-permute-start | bytes 589832 | tf_op jit(solution)/shard_map/ppermute | solution.py:21
  11.7 16.7 %collective-permute-start = (bf16[1,64,1536]{2,1,0:T(8,128)(2,1)}, bf16[1,64,1536]{2,1,0:T(8,128)(2,1)}, u32[]{:S(2)}, u32[]{:S(2)}) collective-permute-start(bf16[1,64,1536]{2,1,0:T(8,128)(2,1)} %get-tuple-element.11), channel_id=1, source_target_pairs={{0,2},{2,4},{4,6},{6,8},{8,10},{10,12},{12,14},{1,3},{3,5},{5,7},{... | collective-permute-start | bytes 589832 | tf_op jit(solution)/shard_map/ppermute | solution.py:19
  35.6 5.3 %copy-start = (bf16[1,512,1536]{1,2,0:T(8,128)(2,1)}, bf16[1,512,1536]{1,2,0:T(8,128)(2,1)S(1)}, u32[]{:S(2)}) copy-start(bf16[1,512,1536]{1,2,0:T(8,128)(2,1)S(1)} %copy.34) | copy-start | bytes 4718596
  35.6 2.1 copy-start.2
  35.6 3.0 %copy-start.4 = (f32[32,512,48]{1,2,0:T(8,128)S(1)}, f32[32,512,48]{1,2,0:T(8,128)}, u32[]{:S(2)}) copy-start(f32[32,512,48]{1,2,0:T(8,128)} %fusion.29) | copy-start | bytes 9437188
  40.9 3.7 %copy-start.10 = (bf16[1,512,1536]{2,1,0:T(8,128)(2,1)S(1)}, bf16[1,512,1536]{2,1,0:T(8,128)(2,1)}, u32[]{:S(2)}) copy-start(bf16[1,512,1536]{2,1,0:T(8,128)(2,1)} %param.9) | copy-start | bytes 4718596
  53.3 4.4 %copy-start.1 = (bf16[1,512,1536]{1,2,0:T(8,128)(2,1)S(1)}, bf16[1,512,1536]{1,2,0:T(8,128)(2,1)}, u32[]{:S(2)}) copy-start(bf16[1,512,1536]{1,2,0:T(8,128)(2,1)} %copy-done) | copy-start | bytes 4718596
  57.7 3.5 %copy-start.9 = (f32[32,48,48]{2,1,0:T(8,128)S(1)}, f32[32,48,48]{2,1,0:T(8,128)}, u32[]{:S(2)}) copy-start(f32[32,48,48]{2,1,0:T(8,128)} %fusion.26) | copy-start | bytes 884740
  57.7 4.5 %copy-start.8 = (f32[32,48,48]{2,1,0:T(8,128)S(1)}, f32[32,48,48]{2,1,0:T(8,128)}, u32[]{:S(2)}) copy-start(f32[32,48,48]{2,1,0:T(8,128)} %fusion.27) | copy-start | bytes 884740
  64.5 209.1 %reduce-scatter.2.cloned.1.call-start = ((), (), s32[]{:S(2)}) async-start(), calls=%async_computation.1 | async-start | bytes 10027008 | tf_op jit(solution)/shard_map/reduce_scatter | solution.py:114
  73.2 1.4 copy-start.5
  74.6 15.7 %collective-permute-start.3 = (bf16[1,64,1536]{2,1,0:T(8,128)(2,1)S(1)}, bf16[1,64,1536]{2,1,0:T(8,128)(2,1)S(1)}, u32[]{:S(2)}, u32[]{:S(2)}) collective-permute-start(bf16[1,64,1536]{2,1,0:T(8,128)(2,1)S(1)} %get-tuple-element.6), channel_id=1, source_target_pairs={{0,2},{2,4},{4,6},{6,8},{8,10},{10,12},{12,14},{1,3},{3,5},{5,7},{... | collective-permute-start | bytes 589832 | tf_op jit(solution)/shard_map/ppermute | solution.py:19
  78.8 9.2 %copy-start.7 = (bf16[1,48,1536]{1,2,0:T(8,128)(2,1)S(1)}, bf16[1,48,1536]{1,2,0:T(8,128)(2,1)}, u32[]{:S(2)}) copy-start(bf16[1,48,1536]{1,2,0:T(8,128)(2,1)} %copy.37) | copy-start | bytes 442372
  78.8 11.5 %collective-permute-start.2 = (bf16[1,64,1536]{2,1,0:T(8,128)(2,1)S(1)}, bf16[1,64,1536]{2,1,0:T(8,128)(2,1)S(1)}, u32[]{:S(2)}, u32[]{:S(2)}) collective-permute-start(bf16[1,64,1536]{2,1,0:T(8,128)(2,1)S(1)} %get-tuple-element.7), channel_id=1, source_target_pairs={{2,0},{4,2},{6,4},{8,6},{10,8},{12,10},{14,12},{3,1},{5,3},{7,5},{... | collective-permute-start | bytes 589832 | tf_op jit(solution)/shard_map/ppermute | solution.py:21
  95.0 2.0 copy-start.3
  95.0 2.5 copy-start.6
Sparse Core Ops, SparseCore 0:
  64.6 94.4 all-reduce.1
  163.2 110.3 reduce-scatter.1
where the time goes:
time: 283 us; the launch traced here: 282 us
  waiting for transfers between devices  166 us (59%)
  matrix products  42.8 us (15%)
  local copies, waits for them, and re-layouts  29.9 us (11%)
  other arithmetic  15.1 us (5%)
  between operations  14.9 us (5%)
  starting transfers between devices  13.3 us (5%)
    reduce_scatter x1, waiting for transfers between devices, on_device(): lax.psum_scatter(lax.dot_general(act_rows, cot_rows, (((0,), (0,)), ((),...  112 us
    psum x1, waiting for transfers between devices, on_device(): grad_conv = lax.psum(conv_local, ('seq', 'rep')) * scale  53.9 us
    ppermute x2, starting transfers between devices, with_halo(): lax.ppermute(tail, axis, [(i, (i + 1) % count) for i in range(ends)])  10.4 us
    dot_general x1, matrix products, on_device(): lax.dot_general(act_rows, cot_rows, (((0,), (0,)), ((), ())), preferred_e...  8.65 us
    dot_general x1, matrix products, on_device(): jnp.dot(act_rows, point_weight, preferred_element_type=jnp.float32)  7.61 us
    dot_general x3, matrix products, conv_taps(): jnp.einsum('slgi,igj->slgj', segment_window, wk, preferred_element_type=j...  7.38 us
    dot_general x1, matrix products, on_device(): lax.dot_general(cot_rows, point_weight, (((1,), (1,)), ((), ())), preferr...  6.98 us
    slice x4, local copies, waits for them, and re-layouts, conv_taps(): weight[kernel_offset].reshape(GROUP_CHANNELS, group_count, GROUP_CHANNELS)  6.61 us
  transfers between devices with their start and end apart: 6, of which 2 were waited for; matrix products, arithmetic and copies ran while one was open for 16% of the time, Pallas kernels for 0%

commit v1 on v0

--- a/solution.py
+++ b/solution.py
@@ -109,7 +109,7 @@
     padded_gradient = with_halo(preactivation_gradient, (("seq", 1),), DILATION_STEP)
     spread = transpose_taps(padded_gradient, conv_weight, local_bins)
     conv_local = weight_taps(padded_input, preactivation_gradient, local_bins)
-    grad_conv = lax.psum(conv_local, ("seq", "rep")) * scale
+    grad_conv = jnp.sum(lax.all_gather(conv_local, ("seq", "rep")), axis=0) * scale
     grad_inputs = (cotangent.astype(jnp.float32) + mask3 * spread).astype(jnp.bfloat16)
     grad_point = lax.psum_scatter(
         lax.dot_general(

time: 283 us -> 293 us (1.035)
  other arithmetic: 15.1 us -> 21.2 us
  local copies, waits for them, and re-layouts: 29.9 us -> 35.4 us
  matrix products: 42.8 us -> 39.1 us
    all_gather x0 -> x1, waiting for transfers between devices: none -> 112 us  [on_device(): lax.all_gather(conv_local, ('seq', 'rep'))]
    reduce_scatter x1, waiting for transfers between devices: 112 us -> 55 us  [on_device(): lax.psum_scatter(lax.dot_general(act_rows, cot_rows, (((0,), (0,)), ((),...]
    psum x1 -> x0, waiting for transfers between devices: 53.9 us -> none  [on_device(): grad_conv = lax.psum(conv_local, ('seq', 'rep')) * scale]
    reduce_sum x0 -> x1, other arithmetic: none -> 6.52 us  [on_device(): jnp.sum(lax.all_gather(conv_local, ('seq', 'rep')), axis=0) * scale]
    dot_general x1, matrix products: 8.65 us -> 5.04 us  [on_device(): lax.dot_general(act_rows, cot_rows, (((0,), (0,)), ((), ())), preferred_e...]
    unnamed x22 -> x20, local copies, waits for them, and re-layouts: 3.15 us -> 6.74 us
    another operation x3, local copies, waits for them, and re-layouts: 3.29 us -> 6.48 us  [weight_taps(): return jnp.stack(taps)]
  transfers between devices with their start and end apart: 6 -> 6, of which waited for: 2 -> 3; matrix products, arithmetic and copies ran while one was open for 16% -> 22% of each run, Pallas kernels for 0% -> 0%
where the time goes in v1:
time: 293 us
  waiting for transfers between devices  168 us (57%)
  matrix products  39.1 us (13%)
  local copies, waits for them, and re-layouts  35.4 us (12%)
  other arithmetic  21.2 us (7%)
  between operations  14.9 us (5%)
  starting transfers between devices  13.6 us (5%)
    all_gather x1, waiting for transfers between devices, on_device(): lax.all_gather(conv_local, ('seq', 'rep'))  112 us
    reduce_scatter x1, waiting for transfers between devices, on_device(): lax.psum_scatter(lax.dot_general(act_rows, cot_rows, (((0,), (0,)), ((),...  55 us
    ppermute x2, starting transfers between devices, with_halo(): lax.ppermute(tail, axis, [(i, (i + 1) % count) for i in range(ends)])  10.7 us
    dot_general x1, matrix products, on_device(): jnp.dot(act_rows, point_weight, preferred_element_type=jnp.float32)  7.55 us
    dot_general x3, matrix products, weight_taps(): jnp.einsum('slgi,slgj->igj', segment_window, grouped, preferred_element_t...  7.55 us
    dot_general x1, matrix products, on_device(): lax.dot_general(cot_rows, point_weight, (((1,), (1,)), ((), ())), preferr...  6.99 us
    unnamed x20, local copies, waits for them, and re-layouts  6.74 us
    reduce_sum x1, other arithmetic, on_device(): jnp.sum(lax.all_gather(conv_local, ('seq', 'rep')), axis=0) * scale  6.52 us
  transfers between devices with their start and end apart: 6, of which 3 were waited for; matrix products, arithmetic and copies ran while one was open for 22% of the time, Pallas kernels for 0%

profile of v1, /device:TPU:0, one launch (start us, length us, event | category | flops | bytes accessed | tf_op | source)
XLA Modules:
  0.0 292.6 jit_solution(11131997874416077689)
XLA Ops:
  11.7 6.2 %collective-permute-start = (bf16[1,64,1536]{2,1,0:T(8,128)(2,1)}, bf16[1,64,1536]{2,1,0:T(8,128)(2,1)}, u32[]{:S(2)}, u32[]{:S(2)}) collective-permute-start(bf16[1,64,1536]{2,1,0:T(8,128)(2,1)} %get-tuple-element.15), channel_id=1, source_target_pairs={{0,2},{2,4},{4,6},{6,8},{8,10},{10,12},{12,14},{1,3},{3,5},{5,7},{... | collective-permute-start | bytes 589832 | tf_op jit(solution)/shard_map/ppermute | solution.py:19
  23.3 3.2 %fusion.29 = f32[32,512,48]{1,2,0:T(8,128)} fusion(bf16[48,32,48]{0,2,1:T(8,128)(2,1)} %bitcast.92, bf16[512,32,48]{0,2,1:T(8,128)(2,1)S(1)} %bitcast.75), kind=kOutput, calls=%fused_computation.48 | convolution fusion | flops 75497472 | bytes 4866048 | tf_op jit(solution)/shard_map/slgi,igj->slgj/dot_general | solution.py:44
  26.5 2.9 %pad_maximum_fusion.2 = (bf16[1,512,1536]{2,1,0:T(8,128)(2,1)}, bf16[1,512,1536]{2,1,0:T(8,128)(2,1)}) fusion(bf16[1,64,1536]{2,1,0:T(8,128)(2,1)} %collective-permute-done.1, bf16[1,512,1536]{2,1,0:T(8,128)(2,1)S(1)} %fusion.1, bf16[1,64,1536]{2,1,0:T(8,128)(2,1)} %collective-permute-done), kind=kLoop, calls=%fused_computation.21 | loop fusion | flops 6291456 | bytes 5111808 | tf_op jit(solution)/shard_map/concatenate | solution.py:17
  31.2 3.2 %copy.53 = bf16[1,512,1536]{1,2,0:T(8,128)(2,1)} copy(bf16[1,512,1536]{2,1,0:T(8,128)(2,1)} %get-tuple-element.12) | data formatting | bytes 3145728 | tf_op jit(solution)/shard_map/slice | solution.py:40
  39.1 5.0 %fusion.8 = f32[1536,1536]{1,0:T(8,128)} fusion(bf16[1,512,1536]{2,1,0:T(8,128)(2,1)S(1)} %copy-done.8, f32[1,512,1,1,1,1,1536]{1,6,5,4,3,2,0:T(8,128)S(1)} %bitcast.81, f32[512]{0:T(512)S(1)} %fusion.16), kind=kOutput, calls=%fused_computation.23 | convolution fusion | flops 2420637696 | bytes 14157824 | tf_op jit(solution)/shard_map/dot_general | solution.py:115
  44.2 3.6 %copy.56 = f32[512,1536]{1,0:T(8,128)} copy(f32[512,1536]{0,1:T(8,128)} %bitcast.82) | data formatting | bytes 6291456 | tf_op jit(solution)/shard_map/reshape | solution.py:47
  47.8 7.0 %fusion.7 = bf16[512,1536]{1,0:T(8,128)(2,1)} fusion(f32[512,1536]{1,0:T(8,128)} %copy.56, bf16[1536,1536]{1,0:T(8,128)(2,1)} %param.8, bf16[1,512,1536]{2,1,0:T(8,128)(2,1)S(1)} %copy-done.8, f32[512]{0:T(512)S(1)} %fusion.16), kind=kOutput, calls=%fused_computation.18 | convolution fusion | flops 2424569856 | bytes 11012096 | tf_op jit(solution)/shard_map/dot_general | solution.py:105
  56.7 3.0 %fusion.27 = f32[32,48,48]{2,1,0:T(8,128)} fusion(bf16[512,32,48]{0,2,1:T(8,128)(2,1)S(1)} %bitcast.70, bf16[512,32,48]{0,2,1:T(8,128)(2,1)} %bitcast.79), kind=kOutput, calls=%fused_computation.46 | convolution fusion | flops 75497472 | bytes 3440640 | tf_op jit(solution)/shard_map/slgi,slgj->igj/dot_general | solution.py:79
  59.7 2.2 copy.69
  63.3 2.2 copy.68
  65.5 3.1 %fusion.25 = f32[32,48,48]{2,1,0:T(8,128)} fusion(bf16[512,32,48]{0,2,1:T(8,128)(2,1)S(1)} %bitcast.72, bf16[512,32,48]{0,2,1:T(8,128)(2,1)} %bitcast.78), kind=kOutput, calls=%fused_computation.44 | convolution fusion | flops 75497472 | bytes 3440640 | tf_op jit(solution)/shard_map/slgi,slgj->igj/dot_general | solution.py:79
  68.6 2.1 copy.67
  70.7 2.1 pad_maximum_fusion.4
  72.9 4.5 %collective-permute-start.3 = (bf16[1,64,1536]{2,1,0:T(8,128)(2,1)S(1)}, bf16[1,64,1536]{2,1,0:T(8,128)(2,1)S(1)}, u32[]{:S(2)}, u32[]{:S(2)}) collective-permute-start(bf16[1,64,1536]{2,1,0:T(8,128)(2,1)S(1)} %get-tuple-element.10), channel_id=1, source_target_pairs={{0,2},{2,4},{4,6},{6,8},{8,10},{10,12},{12,14},{1,3},{3,5},{5,7},{... | collective-permute-start | bytes 589832 | tf_op jit(solution)/shard_map/ppermute | solution.py:19
  79.0 7.6 %fusion.2 = bf16[1,512,1536]{2,1,0:T(8,128)(2,1)} fusion(bf16[1,512,1536]{2,1,0:T(8,128)(2,1)} %param.5, bf16[1536,1536]{1,0:T(8,128)(2,1)} %param.8, f32[512,1536]{1,0:T(8,128)} %copy.56, f32[512]{0:T(512)S(1)} %fusion.16), kind=kOutput, calls=%fused_computation.7 | convolution fusion | flops 2422996992 | bytes 11012096 | tf_op jit(solution)/shard_map/dot_general | solution.py:103
  86.6 2.3 fusion.24
  97.7 2.3 add_add_fusion
  100.1 2.4 copy.66
  102.4 3.0 %add_convert_fusion = bf16[1,512,1536]{2,1,0:T(8,128)(2,1)} fusion(f32[1,512,1536]{2,1,0:T(8,128)S(1)} %copy.66, bf16[1,512,1536]{2,1,0:T(8,128)(2,1)} %param.9, f32[512]{0:T(512)S(1)} %fusion.16), kind=kLoop, calls=%fused_computation.13 | loop fusion | flops 3145728 | bytes 6293504 | tf_op jit(solution)/shard_map/convert_element_type | solution.py:113
  105.4 55.0 %reduce-scatter.2.cloned.1.call-done = f32[96,1536]{1,0:T(8,128)} async-done(((f32[1536,1536]{1,0:T(8,128)}), f32[96,1536]{1,0:T(8,128)}) %reduce-scatter.2.cloned.1.call-update) | async-done | bytes 589840 | tf_op jit(solution)/shard_map/reduce_scatter | solution.py:114
  160.4 1.9 broadcast_multiply_fusion.1
  162.4 111.6 %all-gather.3.cloned.1.call-done = f32[48,48,1536]{2,1,0:T(8,128)} async-done(((f32[3,48,1536]{2,1,0:T(8,128)}), f32[48,48,1536]{2,1,0:T(8,128)}) %all-gather.3.cloned.1.call-update) | async-done | bytes 14155792 | tf_op jit(solution)/shard_map/all_gather | solution.py:112
  274.0 6.5 %reduce_sum.9 = f32[3,48,1536]{2,1,0:T(8,128)S(1)} reduce(f32[16,3,48,1536]{3,2,1,0:T(8,128)} %bitcast.74, f32[]{:T(128)} %constant.22.clone.1), dimensions={0}, to_apply=%region_1.0 | reduce | flops 3317760 | bytes 15040516 | tf_op jit(solution)/shard_map/reduce_sum | solution.py:112
  283.0 2.7 copy.71
  (48 shorter events, 32.0 us)
Async XLA Ops:
  7.2 153.3 %reduce-scatter.2.cloned.1.call-start = ((), (), s32[]{:S(2)}) async-start(), calls=%async_computation.1 | async-start | bytes 10027008 | tf_op jit(solution)/shard_map/reduce_scatter | solution.py:114
  10.4 16.1 %collective-permute-start.1 = (bf16[1,64,1536]{2,1,0:T(8,128)(2,1)}, bf16[1,64,1536]{2,1,0:T(8,128)(2,1)}, u32[]{:S(2)}, u32[]{:S(2)}) collective-permute-start(bf16[1,64,1536]{2,1,0:T(8,128)(2,1)} %get-tuple-element.14), channel_id=1, source_target_pairs={{2,0},{4,2},{6,4},{8,6},{10,8},{12,10},{14,12},{3,1},{5,3},{7,5},{... | collective-permute-start | bytes 589832 | tf_op jit(solution)/shard_map/ppermute | solution.py:21
  11.7 14.8 %collective-permute-start = (bf16[1,64,1536]{2,1,0:T(8,128)(2,1)}, bf16[1,64,1536]{2,1,0:T(8,128)(2,1)}, u32[]{:S(2)}, u32[]{:S(2)}) collective-permute-start(bf16[1,64,1536]{2,1,0:T(8,128)(2,1)} %get-tuple-element.15), channel_id=1, source_target_pairs={{0,2},{2,4},{4,6},{6,8},{8,10},{10,12},{12,14},{1,3},{3,5},{5,7},{... | collective-permute-start | bytes 589832 | tf_op jit(solution)/shard_map/ppermute | solution.py:19
  31.2 4.9 %copy-start = (bf16[1,512,1536]{1,2,0:T(8,128)(2,1)}, bf16[1,512,1536]{1,2,0:T(8,128)(2,1)S(1)}, u32[]{:S(2)}) copy-start(bf16[1,512,1536]{1,2,0:T(8,128)(2,1)S(1)} %copy.49) | copy-start | bytes 4718596
  34.3 1.7 copy-start.1
  34.3 2.5 copy-start.3
  36.8 2.3 copy-start.8
  37.5 1.6 copy-start.4
  44.2 229.8 %all-gather.3.cloned.1.call-start = ((), (), s32[]{:S(2)}) async-start(), calls=%async_computation.2 | async-start | bytes 15040512 | tf_op jit(solution)/shard_map/all_gather | solution.py:112
  65.5 7.4 %copy-start.5 = (bf16[512,1536]{1,0:T(8,128)(2,1)S(1)}, bf16[512,1536]{1,0:T(8,128)(2,1)}, u32[]{:S(2)}) copy-start(bf16[512,1536]{1,0:T(8,128)(2,1)} %fusion.7) | copy-start | bytes 4718596
  72.9 16.0 %collective-permute-start.3 = (bf16[1,64,1536]{2,1,0:T(8,128)(2,1)S(1)}, bf16[1,64,1536]{2,1,0:T(8,128)(2,1)S(1)}, u32[]{:S(2)}, u32[]{:S(2)}) collective-permute-start(bf16[1,64,1536]{2,1,0:T(8,128)(2,1)S(1)} %get-tuple-element.10), channel_id=1, source_target_pairs={{0,2},{2,4},{4,6},{6,8},{8,10},{10,12},{12,14},{1,3},{3,5},{5,7},{... | collective-permute-start | bytes 589832 | tf_op jit(solution)/shard_map/ppermute | solution.py:19
  77.4 9.2 %copy-start.7 = (bf16[1,48,1536]{1,2,0:T(8,128)(2,1)S(1)}, bf16[1,48,1536]{1,2,0:T(8,128)(2,1)}, u32[]{:S(2)}) copy-start(bf16[1,48,1536]{1,2,0:T(8,128)(2,1)} %copy.52) | copy-start | bytes 442372
  77.4 13.1 %collective-permute-start.2 = (bf16[1,64,1536]{2,1,0:T(8,128)(2,1)S(1)}, bf16[1,64,1536]{2,1,0:T(8,128)(2,1)S(1)}, u32[]{:S(2)}, u32[]{:S(2)}) collective-permute-start(bf16[1,64,1536]{2,1,0:T(8,128)(2,1)S(1)} %get-tuple-element.11), channel_id=1, source_target_pairs={{2,0},{4,2},{6,4},{8,6},{10,8},{12,10},{14,12},{3,1},{5,3},{7,5},{... | collective-permute-start | bytes 589832 | tf_op jit(solution)/shard_map/ppermute | solution.py:21
  95.2 2.0 copy-start.2
  95.2 2.5 copy-start.6
Sparse Core Ops, SparseCore 0:
  44.3 116.0 reduce-scatter.1
  163.5 110.3 all-gather.2
